TPU v7x, 32 devices: a whole 2x2x4 slice. The times are simulated.
32 devices in a mesh: row: 8 (over y, x, core), col: 4 (over z).
Axes of the slice: x: 2, y: 2, z: 4, core: 2. Of those that a mesh axis runs over, the one named last changes fastest.
Arguments:
- out_grads: bfloat16 [64, 28672], P('col', 'row'), may hold values from -6 to 6
- in_acts: bfloat16 [64, 8192], P('row', 'col'), may hold values from -6 to 6
- out_basis: bfloat16 [28672, 28672], P('row', 'col'), may hold values from -0.03125 to 0.03125
- in_basis: bfloat16 [8192, 8192], P('col', 'row'), may hold values from -0.0625 to 0.0625
- eigenvalues: bfloat16 [28672, 8192], P('col', 'row'), may hold values from 0.019897461 to 2
- queries: bfloat16 [2, 28672, 8192], P(None, 'col', 'row'), may hold values from -0.00015640259 to 0.00015640259
Outputs:
- scores: float32 [2, 64], replicated
All inputs are finite; a program needn't handle non-finite values.
Results may differ from a plain program's by a relative error of at most 0.0045.
Values may be sent and summed in bfloat16 or wider, within the bound.
No kernel may reach another device: no remote copies, remote signals or barrier semaphores. Data moves between devices by JAX's collectives and lax.ppermute only.
A program may use at most 192 MiB of HBM per device.

v0:
```python
import jax
import jax.numpy as jnp
from jax import lax
from jax.sharding import PartitionSpec as P

DAMPING = 0.1


def local(out_grads, in_acts, out_basis, in_basis, eigenvalues, queries):
    grads_all = lax.all_gather(out_grads, "col", axis=0, tiled=True)
    grad_mine = lax.psum_scatter(
        jnp.dot(grads_all, out_basis, preferred_element_type=jnp.float32),
        "row",
        scatter_dimension=0,
        tiled=True,
    ).astype(jnp.bfloat16)
    grad_rot = lax.all_gather(grad_mine, "row", axis=0, tiled=True)
    acts_all = lax.all_gather(in_acts, "row", axis=0, tiled=True)
    act_part = jnp.dot(acts_all, in_basis, preferred_element_type=jnp.float32)
    act_rot = lax.psum(act_part, "col").astype(jnp.bfloat16)
    shifted = eigenvalues.astype(jnp.float32) + DAMPING
    scaled = queries.astype(jnp.float32) / shifted[None]
    lifted = jnp.einsum(
        "qkj,tj->qkt",
        scaled,
        act_rot.astype(jnp.float32),
        precision=lax.Precision.HIGHEST,
        preferred_element_type=jnp.float32,
    )
    partial_scores = jnp.einsum(
        "qkt,tk->qt", lifted, grad_rot.astype(jnp.float32), precision=lax.Precision.HIGHEST
    )
    return lax.psum(partial_scores, ("row", "col"))


def solution(mesh):
    in_specs = (
        P("col", "row"),
        P("row", "col"),
        P("row", "col"),
        P("col", "row"),
        P("col", "row"),
        P(None, "col", "row"),
    )
    out_specs = P()
    return jax.shard_map(local, mesh=mesh, in_specs=in_specs, out_specs=out_specs, check_vma=False)
```

profile of v0, /device:TPU:0, one launch (start us, length us, event | category | flops | bytes accessed | tf_op | source)
XLA Modules:
  0.0 220.7 jit_solution(7782558009660924071)
XLA Ops:
  6.5 0.0 reduce-scatter.2.cloned.1.call-start
  6.5 17.0 %all_gather.9 = bf16[64,3584]{1,0:T(8,128)(2,1)S(1)} all-gather(bf16[16,3584]{1,0:T(8,128)(2,1)} %param.6), channel_id=1, replica_groups=mesh['row'=8,'col'=4] {'col'}, dimensions={0}, use_global_device_ids=true | all-gather | bytes 573440 | tf_op jit(solution)/shard_map/all_gather | solution.py:10
  23.5 21.8 %fusion.7 = f32[64,7168]{1,0:T(8,128)} fusion(bf16[64,3584]{1,0:T(8,128)(2,1)S(1)} %all_gather.9, bf16[3584,7168]{1,0:T(8,128)(2,1)} %param.8), kind=kOutput, calls=%fused_computation.9 | convolution fusion | flops 3288334336 | bytes 53673984 | tf_op jit(solution)/shard_map/dot_general | solution.py:12
  45.3 0.0 copy-start.1
  45.3 0.0 reduce-scatter.2.cloned.1.call-update
  45.4 0.0 copy-start
  45.4 17.4 %convert_add_fusion = f32[7168,1024]{1,0:T(8,128)} fusion(bf16[7168,1024]{1,0:T(8,128)(2,1)} %param.10), kind=kLoop, calls=%fused_computation.3 | loop fusion | flops 14680064 | bytes 44040192 | tf_op jit(solution)/shard_map/add | solution.py:21
  62.8 0.0 copy-done.1
  62.8 9.4 %all_gather.11 = bf16[64,2048]{1,0:T(8,128)(2,1)S(1)} all-gather(bf16[8,2048]{1,0:T(8,128)(2,1)S(1)} %copy-done.1), channel_id=1, replica_groups=mesh['row'=8,'col'=4] {'row'}, dimensions={0}, use_global_device_ids=true | all-gather | bytes 294912 | tf_op jit(solution)/shard_map/all_gather | solution.py:18
  72.2 0.0 copy-done
  72.2 0.8 fusion.8
  73.1 25.6 %all-reduce.1 = bf16[64,1024]{1,0:T(8,128)(2,1)S(1)} all-reduce(f32[64,1024]{1,0:T(8,128)S(1)} %fusion.8), channel_id=1, replica_groups=mesh['row'=8,'col'=4] {'col'}, use_global_device_ids=true, to_apply=%region_1.0 | all-reduce | flops 65536 | bytes 393216 | tf_op jit(solution)/shard_map/psum | solution.py:20
  98.7 45.4 %fusion = f32[2,7168,64]{1,2,0:T(8,128)} fusion(bf16[2,7168,1024]{2,1,0:T(8,128)(2,1)} %param.11, f32[7168,1024]{1,0:T(8,128)} %convert_add_fusion, bf16[64,1024]{1,0:T(8,128)(2,1)S(1)} %all-reduce.1), kind=kOutput, calls=%fused_computation.1 | convolution fusion | flops 11303649280 | bytes 62521344 | tf_op jit(solution)/shard_map/qkj,tj->qkt/dot_general | solution.py:23
  144.1 0.0 reduce-scatter.2.cloned.1.call-done
  144.1 1.0 convert_element_type.14
  145.1 11.0 %all_gather.10 = bf16[64,7168]{1,0:T(8,128)(2,1)S(1)} all-gather(bf16[8,7168]{1,0:T(8,128)(2,1)S(1)} %convert_element_type.14), channel_id=1, replica_groups=mesh['row'=8,'col'=4] {'row'}, dimensions={0}, use_global_device_ids=true | all-gather | bytes 1032192 | tf_op jit(solution)/shard_map/all_gather | solution.py:17
  156.0 19.9 %fusion.2 = f32[64,1,2]{2,1,0:T(1,128)S(1)} fusion(f32[2,7168,64]{1,2,0:T(8,128)} %fusion, bf16[64,7168,1]{1,0,2:T(8,128)(2,1)S(1)} %bitcast.11), kind=kOutput, calls=%fused_computation.4 | convolution fusion | flops 11010048 | bytes 4588032 | tf_op jit(solution)/shard_map/qkt,tk->qt/dot_general | solution.py:30
  175.9 0.1 copy.9
  176.0 37.8 %psum.15 = f32[2,64]{1,0:T(2,128)} all-reduce(f32[2,64]{1,0:T(2,128)S(1)} %bitcast.12), channel_id=1, replica_groups=mesh['row'=8,'col'=4] {'row','col'}, use_global_device_ids=true, to_apply=%region_2.0 | all-reduce | flops 128 | bytes 1024 | tf_op jit(solution)/shard_map/psum | solution.py:33
Async XLA Ops:
  6.5 137.6 %reduce-scatter.2.cloned.1.call-start = ((), (), s32[]{:S(2)}) async-start(), calls=%async_computation.1 | async-start | bytes 2064384 | tf_op jit(solution)/shard_map/reduce_scatter | solution.py:11
  45.3 17.4 %copy-start.1 = (bf16[8,2048]{1,0:T(8,128)(2,1)S(1)}, bf16[8,2048]{1,0:T(8,128)(2,1)}, u32[]{:S(2)}) copy-start(bf16[8,2048]{1,0:T(8,128)(2,1)} %param.7) | copy-start | bytes 98308
  45.4 26.8 %copy-start = (bf16[2048,1024]{1,0:T(8,128)(2,1)S(1)}, bf16[2048,1024]{1,0:T(8,128)(2,1)}, u32[]{:S(2)}) copy-start(bf16[2048,1024]{1,0:T(8,128)(2,1)} %param.9) | copy-start | bytes 12582916
Sparse Core Ops, SparseCore 0:
  45.5 42.0 reduce-scatter.1
where the time goes:
time: 221 us
  blocking collectives  101 us (46%)
  matrix products  88 us (40%)
  other arithmetic  18.3 us (8%)
  between operations  13.4 us (6%)
    dot_general x1, matrix products, local(): jnp.einsum('qkj,tj->qkt', scaled, act_rot.astype(jnp.float32), precision=...  45.4 us
    psum x1, blocking collectives, local(): return lax.psum(partial_scores, ('row', 'col'))  37.8 us
    psum x1, blocking collectives, local(): act_rot = lax.psum(act_part, 'col').astype(jnp.bfloat16)  25.6 us
    dot_general x1, matrix products, local(): jnp.dot(grads_all, out_basis, preferred_element_type=jnp.float32)  21.8 us
    dot_general x1, matrix products, local(): jnp.einsum('qkt,tk->qt', lifted, grad_rot.astype(jnp.float32), precision=...  19.9 us
    add x1, other arithmetic, local(): shifted = eigenvalues.astype(jnp.float32) + DAMPING  17.4 us
    all_gather x1, blocking collectives, local(): grads_all = lax.all_gather(out_grads, 'col', axis=0, tiled=True)  17 us
    all_gather x1, blocking collectives, local(): grad_rot = lax.all_gather(grad_mine, 'row', axis=0, tiled=True)  11 us
  transfers between devices with their start and end apart: 1, of which 0 were waited for; matrix products, arithmetic and copies ran while one was open for 29% of the time, Pallas kernels for 0%

commit v1 on v0

--- a/solution.py
+++ b/solution.py
@@ -17,7 +17,7 @@
     grad_rot = lax.all_gather(grad_mine, "row", axis=0, tiled=True)
     acts_all = lax.all_gather(in_acts, "row", axis=0, tiled=True)
     act_part = jnp.dot(acts_all, in_basis, preferred_element_type=jnp.float32)
-    act_rot = lax.psum(act_part, "col").astype(jnp.bfloat16)
+    act_rot = jnp.sum(lax.all_gather(act_part, "col"), axis=0).astype(jnp.bfloat16)
     shifted = eigenvalues.astype(jnp.float32) + DAMPING
     scaled = queries.astype(jnp.float32) / shifted[None]
     lifted = jnp.einsum(

time: 221 us -> 205 us (0.928)
  blocking collectives: 101 us -> 79.3 us
  matrix products: 88 us -> 91.1 us
    psum x1 -> x0, blocking collectives: 25.6 us -> none  [local(): act_rot = lax.psum(act_part, 'col').astype(jnp.bfloat16)]
    all_gather x1, blocking collectives: 17 us -> 20 us  [local(): grads_all = lax.all_gather(out_grads, 'col', axis=0, tiled=True)]
    dot_general x1, matrix products: 0.85 us -> 3.72 us  [local(): act_part = jnp.dot(acts_all, in_basis, preferred_element_type=jnp.float32)]
  transfers between devices with their start and end apart: 1 -> 2, of which waited for: 0 -> 0; matrix products, arithmetic and copies ran while one was open for 29% -> 42% of each run, Pallas kernels for 0% -> 0%
where the time goes in v1:
time: 205 us
  matrix products  91.1 us (44%)
  blocking collectives  79.3 us (39%)
  other arithmetic  19.2 us (9%)
  between operations  14.8 us (7%)
    dot_general x1, matrix products, local(): jnp.einsum('qkj,tj->qkt', scaled, act_rot.astype(jnp.float32), precision=...  45.7 us
    psum x1, blocking collectives, local(): return lax.psum(partial_scores, ('row', 'col'))  37.9 us
    dot_general x1, matrix products, local(): jnp.dot(grads_all, out_basis, preferred_element_type=jnp.float32)  21.8 us
    all_gather x1, blocking collectives, local(): grads_all = lax.all_gather(out_grads, 'col', axis=0, tiled=True)  20 us
    dot_general x1, matrix products, local(): jnp.einsum('qkt,tk->qt', lifted, grad_rot.astype(jnp.float32), precision=...  19.9 us
    add x1, other arithmetic, local(): shifted = eigenvalues.astype(jnp.float32) + DAMPING  17 us
    all_gather x1, blocking collectives, local(): acts_all = lax.all_gather(in_acts, 'row', axis=0, tiled=True)  11 us
    all_gather x1, blocking collectives, local(): grad_rot = lax.all_gather(grad_mine, 'row', axis=0, tiled=True)  10.4 us
  transfers between devices with their start and end apart: 2, of which 0 were waited for; matrix products, arithmetic and copies ran while one was open for 42% of the time, Pallas kernels for 0%

profile of v1, /device:TPU:0, one launch (start us, length us, event | category | flops | bytes accessed | tf_op | source)
XLA Modules:
  0.0 204.7 jit_solution(4999511553947791724)
XLA Ops:
  7.4 0.0 all-gather.3.cloned.1.call-start
  7.4 11.0 %all_gather.17 = bf16[64,2048]{1,0:T(8,128)(2,1)S(1)} all-gather(bf16[8,2048]{1,0:T(8,128)(2,1)} %param.7), channel_id=1, replica_groups=mesh['row'=8,'col'=4] {'row'}, dimensions={0}, use_global_device_ids=true | all-gather | bytes 294912 | tf_op jit(solution)/shard_map/all_gather | solution.py:18
  18.3 3.7 %fusion.8 = f32[64,1024]{1,0:T(8,128)} fusion(bf16[64,2048]{1,0:T(8,128)(2,1)S(1)} %all_gather.17, bf16[2048,1024]{1,0:T(8,128)(2,1)} %param.9), kind=kOutput, calls=%fused_computation.10 | convolution fusion | flops 268435456 | bytes 4718592 | tf_op jit(solution)/shard_map/dot_general | solution.py:19
  22.1 0.0 all-gather.3.cloned.1.call-update
  22.1 0.0 reduce-scatter.2.cloned.1.call-start
  22.1 20.0 %all_gather.15 = bf16[64,3584]{1,0:T(8,128)(2,1)S(1)} all-gather(bf16[16,3584]{1,0:T(8,128)(2,1)} %param.6), channel_id=1, replica_groups=mesh['row'=8,'col'=4] {'col'}, dimensions={0}, use_global_device_ids=true | all-gather | bytes 573440 | tf_op jit(solution)/shard_map/all_gather | solution.py:10
  42.1 21.8 %fusion.7 = f32[64,7168]{1,0:T(8,128)} fusion(bf16[64,3584]{1,0:T(8,128)(2,1)S(1)} %all_gather.15, bf16[3584,7168]{1,0:T(8,128)(2,1)} %param.8), kind=kOutput, calls=%fused_computation.9 | convolution fusion | flops 3288334336 | bytes 53673984 | tf_op jit(solution)/shard_map/dot_general | solution.py:12
  64.0 0.0 reduce-scatter.2.cloned.1.call-update
  64.0 17.0 %convert_add_fusion = f32[7168,1024]{1,0:T(8,128)} fusion(bf16[7168,1024]{1,0:T(8,128)(2,1)} %param.10), kind=kLoop, calls=%fused_computation.3 | loop fusion | flops 14680064 | bytes 44040192 | tf_op jit(solution)/shard_map/add | solution.py:21
  81.0 0.0 all-gather.3.cloned.1.call-done
  81.0 1.3 reduce_sum.9
  82.3 45.7 %fusion = f32[2,7168,64]{1,2,0:T(8,128)} fusion(bf16[2,7168,1024]{2,1,0:T(8,128)(2,1)} %param.11, f32[7168,1024]{1,0:T(8,128)} %convert_add_fusion, bf16[64,1024]{1,0:T(8,128)(2,1)S(1)} %reduce_sum.9), kind=kOutput, calls=%fused_computation.1 | convolution fusion | flops 11303649280 | bytes 62521344 | tf_op jit(solution)/shard_map/qkj,tj->qkt/dot_general | solution.py:23
  128.0 0.0 reduce-scatter.2.cloned.1.call-done
  128.0 1.0 convert_element_type.14
  128.9 10.4 %all_gather.16 = bf16[64,7168]{1,0:T(8,128)(2,1)S(1)} all-gather(bf16[8,7168]{1,0:T(8,128)(2,1)S(1)} %convert_element_type.14), channel_id=1, replica_groups=mesh['row'=8,'col'=4] {'row'}, dimensions={0}, use_global_device_ids=true | all-gather | bytes 1032192 | tf_op jit(solution)/shard_map/all_gather | solution.py:17
  139.3 19.9 %fusion.2 = f32[64,1,2]{2,1,0:T(1,128)S(1)} fusion(f32[2,7168,64]{1,2,0:T(8,128)} %fusion, bf16[64,7168,1]{1,0,2:T(8,128)(2,1)S(1)} %bitcast.13), kind=kOutput, calls=%fused_computation.4 | convolution fusion | flops 11010048 | bytes 4588032 | tf_op jit(solution)/shard_map/qkt,tk->qt/dot_general | solution.py:30
  159.2 0.1 copy.9
  159.3 37.9 %psum.7 = f32[2,64]{1,0:T(2,128)} all-reduce(f32[2,64]{1,0:T(2,128)S(1)} %bitcast.14), channel_id=1, replica_groups=mesh['row'=8,'col'=4] {'row','col'}, use_global_device_ids=true, to_apply=%region_2.0 | all-reduce | flops 128 | bytes 1024 | tf_op jit(solution)/shard_map/psum | solution.py:33
Async XLA Ops:
  7.4 73.6 %all-gather.3.cloned.1.call-start = ((), (), s32[]{:S(2)}) async-start(), calls=%async_computation.2 | async-start | bytes 1310720 | tf_op jit(solution)/shard_map/all_gather | solution.py:20
  22.1 105.9 %reduce-scatter.2.cloned.1.call-start = ((), (), s32[]{:S(2)}) async-start(), calls=%async_computation.1 | async-start | bytes 2064384 | tf_op jit(solution)/shard_map/reduce_scatter | solution.py:11
Sparse Core Ops, SparseCore 0:
  22.2 31.5 all-gather.2
Sparse Core Ops, SparseCore 1:
  64.1 38.0 reduce-scatter.1
